TPU v7x, 128 devices: a whole 4x4x4 slice. The times are simulated.
128 devices in a mesh: dp: 32 (over y, x, core), mp: 4 (over z).
Axes of the slice: x: 4, y: 4, z: 4, core: 2. Of those that a mesh axis runs over, the one named last changes fastest.
Arguments:
- hidden: bfloat16 [4096, 2560], P('dp', 'mp'), may hold values from -6 to 6
- norm_gain: bfloat16 [2560], replicated, may hold values from 0.5 to 1.5
- shared_gate: bfloat16 [2560, 3072], P(None, 'mp'), may hold values from -0.125 to 0.125
- shared_up: bfloat16 [2560, 3072], P(None, 'mp'), may hold values from -0.125 to 0.125
- shared_down: bfloat16 [3072, 2560], P('mp'), may hold values from -0.109375 to 0.109375
- expert_gate: bfloat16 [64, 2560, 1536], P('dp', None, 'mp'), may hold values from -0.125 to 0.125
- expert_up: bfloat16 [64, 2560, 1536], P('dp', None, 'mp'), may hold values from -0.125 to 0.125
- expert_down: bfloat16 [64, 1536, 2560], P('dp', 'mp'), may hold values from -0.15625 to 0.15625
- adapter_in: bfloat16 [64, 3072, 16], P('dp', 'mp'), may hold values from -0.109375 to 0.109375
- adapter_out: bfloat16 [64, 16, 2560], P('dp'), may hold values from -1.5 to 1.5
- active: int32 [16], replicated, may hold values from 0 to 63, as said below
- lengths: int32 [64], replicated, may hold values from 1 to 1024, 4096 in all
- request_adapter: int32 [64], replicated, may hold values from 0 to 15
- routes: int32 [4096, 6], P('dp'), may hold values from 0 to 63, all different within a row; in each aligned block of 128 rows (0 to 127, 128 to 255, ...) at most 16 rows name the same one
- route_weights: float32 [4096, 6], P('dp'), may hold values from 0.05 to 0.35
Outputs:
- layer_out: bfloat16 [4096, 2560], P('dp', 'mp')
Inputs may be any that keep to these rules, and one draw needn't show every extreme that they name: `active`: the entries are distinct. `routes`: within the 128 rows of one index of dp no expert is named more than 16 times, and that many is reached; a row names distinct experts.
All inputs are finite; a program needn't handle non-finite values.
Results may differ from a plain program's by a relative error of at most 0.015.
Values may be sent and summed in bfloat16 or wider, within the bound.
No kernel may reach another device: no remote copies, remote signals or barrier semaphores. Data moves between devices by JAX's collectives and lax.ppermute only.
A program may use at most 128 MiB of HBM per device.

v0:
```python
import jax
import jax.numpy as jnp
from jax import lax
from jax.sharding import PartitionSpec as P


def experts_apply(slots_in, expert_gate, expert_up, expert_down):
    gate_val = jnp.einsum(
        "sjcd,jdf->sjcf", slots_in, expert_gate, preferred_element_type=jnp.float32
    )
    up_val = jnp.einsum("sjcd,jdf->sjcf", slots_in, expert_up, preferred_element_type=jnp.float32)
    inner = (jax.nn.silu(gate_val) * up_val).astype(jnp.bfloat16)
    return jnp.einsum("sjcf,jfd->sjcd", inner, expert_down, preferred_element_type=jnp.float32)


def body(
    hidden,
    norm_gain,
    shared_gate,
    shared_up,
    shared_down,
    expert_gate,
    expert_up,
    expert_down,
    adapter_in,
    adapter_out,
    active,
    lengths,
    request_adapter,
    routes,
    route_weights,
):
    tok_rows = routes.shape[0]
    top_count = routes.shape[1]
    dp_count = lax.axis_size("dp")
    mp_count = lax.axis_size("mp")
    dp_index = lax.axis_index("dp")
    local_experts = expert_gate.shape[0]
    total_experts = local_experts * dp_count
    capacity = mp_count * max(1, tok_rows * top_count * 4 // (total_experts * mp_count * 3))
    gathered = lax.all_gather(hidden, "mp", axis=1, tiled=True)
    values = gathered.astype(jnp.float32)
    factor = lax.rsqrt(jnp.mean(values * values, axis=-1, keepdims=True) + 1e-06)
    normed = (values * factor * norm_gain.astype(jnp.float32)).astype(jnp.bfloat16)
    width = normed.shape[1]
    shared_lin = jnp.dot(normed, shared_gate, preferred_element_type=jnp.float32)
    shared_pre = jnp.dot(normed, shared_up, preferred_element_type=jnp.float32)
    shared_act = (jax.nn.silu(shared_lin) * shared_pre).astype(jnp.bfloat16)
    active_count = active.shape[0]
    rank_width = adapter_in.shape[2]
    local_adapters = adapter_in.shape[0]
    owned_ids = dp_index * local_adapters + jnp.arange(local_adapters, dtype=jnp.int32)
    selector = (active[:, None] == owned_ids[None, :]).astype(jnp.bfloat16)
    picked_in = jnp.einsum(
        "ji,isr->jsr", selector, adapter_in, preferred_element_type=jnp.float32
    ).astype(jnp.bfloat16)
    picked_out = jnp.einsum(
        "ji,ird->jrd", selector, adapter_out, preferred_element_type=jnp.float32
    ).astype(jnp.bfloat16)
    picked_in, picked_out = (
        lax.psum(picked_in, "dp").astype(jnp.float32),
        lax.psum(picked_out, "dp").astype(jnp.float32),
    )
    picked_in = picked_in.astype(jnp.bfloat16)
    request_end = jnp.cumsum(lengths)
    positions = dp_index * tok_rows + jnp.arange(tok_rows, dtype=jnp.int32)
    request_of = jnp.sum((request_end[None, :] <= positions[:, None]).astype(jnp.int32), axis=1)
    request_hot = (
        request_of[:, None] == jnp.arange(lengths.shape[0], dtype=jnp.int32)[None, :]
    ).astype(jnp.int32)
    slot_of = jnp.sum(request_hot * request_adapter[None, :], axis=1)
    chosen = (slot_of[:, None] == jnp.arange(active_count, dtype=jnp.int32)[None, :]).astype(
        jnp.float32
    )
    in_matrix = jnp.transpose(picked_in, (1, 0, 2)).reshape(
        shared_act.shape[1], active_count * rank_width
    )
    lowrank = jnp.dot(shared_act, in_matrix, preferred_element_type=jnp.float32)
    lowrank = (lowrank.reshape(tok_rows, active_count, rank_width) * chosen[:, :, None]).reshape(
        tok_rows, active_count * rank_width
    )
    adapted = jnp.dot(
        lowrank,
        picked_out.reshape(active_count * rank_width, width),
        precision=lax.Precision.HIGHEST,
    )
    partial_out = jnp.dot(shared_act, shared_down, preferred_element_type=jnp.float32) + adapted
    flat_routes = routes.reshape(-1)
    flat_weights = route_weights.reshape(-1)
    expert_hot = (
        flat_routes[:, None] == jnp.arange(total_experts, dtype=jnp.int32)[None, :]
    ).astype(jnp.int32)
    earlier = jnp.cumsum(expert_hot, axis=0) - expert_hot
    position = jnp.sum(earlier * expert_hot, axis=1)
    slot_index = flat_routes * capacity + position
    token_of = jnp.arange(tok_rows * top_count, dtype=jnp.int32) // top_count
    send_rows = (
        jnp.zeros((total_experts * capacity, width), jnp.bfloat16)
        .at[slot_index]
        .set(normed[token_of])
    )
    send_rows = send_rows.reshape(dp_count, local_experts, capacity, width)
    returned = lax.all_to_all(
        experts_apply(
            lax.all_to_all(send_rows, "dp", split_axis=0, concat_axis=0, tiled=True),
            expert_gate,
            expert_up,
            expert_down,
        ).astype(jnp.bfloat16),
        "dp",
        split_axis=0,
        concat_axis=0,
        tiled=True,
    ).astype(jnp.float32)
    returned = returned.reshape(total_experts * capacity, width)
    picked_rows = returned[slot_index]
    routed = jnp.sum(
        (picked_rows * flat_weights[:, None]).reshape(tok_rows, top_count, width), axis=1
    )
    partial_out = partial_out + routed
    return lax.psum_scatter(partial_out.astype(jnp.bfloat16), "mp", scatter_dimension=1, tiled=True)


def solution(mesh):
    in_specs = (
        P("dp", "mp"),
        P(),
        P(None, "mp"),
        P(None, "mp"),
        P("mp", None),
        P("dp", None, "mp"),
        P("dp", None, "mp"),
        P("dp", "mp", None),
        P("dp", "mp", None),
        P("dp", None, None),
        P(),
        P(),
        P(),
        P("dp", None),
        P("dp", None),
    )
    out_specs = P("dp", "mp")
    return jax.shard_map(body, mesh=mesh, in_specs=in_specs, out_specs=out_specs, check_vma=False)
```

profile of v0, /device:TPU:0, one launch (start us, length us, event | category | flops | bytes accessed | tf_op | source)
XLA Modules:
  0.0 373.1 jit_solution(8138706086236999893)
XLA Ops:
  6.5 0.8 copy.48
  7.6 0.7 broadcast_multiply_fusion
  8.4 1.8 reduce-window.19
  10.2 0.3 slice_reduce_fusion
  10.8 14.9 %all_gather.3 = bf16[128,2560]{1,0:T(8,128)(2,1)S(1)} all-gather(bf16[128,640]{1,0:T(8,128)(2,1)} %param.15), channel_id=1, replica_groups=mesh['dp'=32,'mp'=4] {'mp'}, dimensions={1}, use_global_device_ids=true | all-gather | bytes 819200 | tf_op jit(solution)/shard_map/all_gather | solution.py:41
  25.9 0.7 convert_element_type.54
  26.8 0.2 fusion.27
  27.0 27.6 %scatter_custom_fusion = bf16[1024,2560]{1,0:T(8,128)(2,1)} fusion(s32[768]{0:T(1024)S(1)} %fusion.40, bf16[128,2560]{1,0:T(8,128)(2,1)S(1)} %fusion.27, s32[1024]{0:T(1024)S(1)} %pad_clamp_fusion.1, bf16[]{:T(256)} %constant.44.clone.1), kind=kCustom, calls=%fused_computation.14 | custom fusion | bytes 5242882 | tf_op jit(solution)/shard_map/scatter | solution.py:100
  54.6 69.7 %all_to_all.10 = bf16[32,2,16,2560]{3,2,1,0:T(8,128)(2,1)S(1)} all-to-all(bf16[32,2,16,2560]{3,2,1,0:T(8,128)(2,1)} %bitcast.96), channel_id=1, replica_groups=mesh['dp'=32,'mp'=4] {'dp'}, dimensions={0} | all-to-all | bytes 10485760 | tf_op jit(solution)/shard_map/all_to_all | solution.py:105
  124.3 2.3 copy-done.2
  126.6 2.9 fusion.3
  129.5 12.8 %fusion = bf16[32,2,16,2560]{3,2,0,1:T(8,128)(2,1)} fusion(bf16[2,384,2560]{2,1,0:T(8,128)(2,1)} %param.22, f32[2,32,16,384]{3,2,1,0:T(8,128)S(1)} %fusion.3, bf16[2,2560,384]{2,1,0:T(8,128)(2,1)} %param.21, bf16[32,2,16,2560]{3,2,1,0:T(8,128)(2,1)} %copy-done.2), kind=kOutput, calls=%fused_computation.6 | convolution fusion | flops 4031512576 | bytes 19922944 | tf_op jit(solution)/shard_map/sjcf,jfd->sjcd/dot_general | solution.py:13
  142.3 5.3 %copy.53 = bf16[32,2,16,2560]{3,2,1,0:T(8,128)(2,1)} copy(bf16[32,2,16,2560]{3,2,0,1:T(8,128)(2,1)} %fusion) | data formatting | bytes 10485760 | tf_op jit(solution)/shard_map/convert_element_type | solution.py:109
  147.6 5.0 %all-to-all-start.1 = ((bf16[32,2,16,2560]{3,2,1,0:T(8,128)(2,1)}), bf16[32,2,16,2560]{3,2,1,0:T(8,128)(2,1)}, u32[]{:S(2)}, u32[]{:S(2)}) async-start(bf16[32,2,16,2560]{3,2,1,0:T(8,128)(2,1)} %copy.53), calls=%async_computation.1 | async-start | bytes 10485760 | tf_op jit(solution)/shard_map/all_to_all | solution.py:103
  152.7 0.4 fusion.29
  153.1 0.9 copy.77
  154.0 1.7 convolution_convert_fusion.1
  155.8 0.3 reduce-scatter.4.cloned.1.call-start
  156.7 2.9 fusion.51
  159.7 0.3 copy-done.9
  160.0 0.7 fusion.30
  160.7 138.1 %all-reduce.3.cloned.1.call-done = (bf16[16,16,768]{2,1,0:T(8,128)(2,1)}, bf16[16,16,2560]{2,0,1:T(8,128)(2,1)}) async-done(((bf16[16,16,768]{2,1,0:T(8,128)(2,1)}, bf16[16,16,2560]{2,0,1:T(8,128)(2,1)}), (bf16[16,16,768]{2,1,0:T(8,128)(2,1)}, bf16[16,16,2560]{2,0,1:T(8,128)(2,1)})) %all-reduce.3.cloned.1.call-update) | async-done | bytes 1703952 | tf_op jit(solution)/shard_map/psum | solution.py:61
  298.8 1.3 convolution_multiply_fusion.1
  300.1 2.6 convolution_bitcast_fusion
  302.8 7.9 %bitcast_convert_fusion = f32[1024,2560]{1,0:T(8,128)} fusion(bf16[32,2,16,2560]{3,2,1,0:T(8,128)(2,1)} %all-to-all-done.1), kind=kLoop, calls=%fused_computation.5 | loop fusion | flops 2621440 | bytes 15728640 | tf_op jit(solution)/shard_map/reshape | solution.py:115
  310.7 12.4 %gather_fusion = f32[768,2560]{1,0:T(8,128)} fusion(f32[1024,2560]{1,0:T(8,128)} %bitcast_convert_fusion, s32[1024]{0:T(1024)S(1)} %pad_clamp_fusion), kind=kCustom, calls=%fused_computation.1 | custom fusion | bytes 15731712 | tf_op jit(solution)/shard_map/gather | solution.py:116
  323.1 9.2 %gather.10 = f32[128,6,2560]{2,1,0:T(8,128)} reshape(f32[768,2560]{1,0:T(8,128)} %gather_fusion) | data formatting | bytes 15728640 | tf_op jit(solution)/shard_map/gather | solution.py:116
  332.3 8.1 %multiply_reduce_fusion = f32[128,2560]{1,0:T(8,128)S(1)} fusion(f32[128,6,2560]{2,1,0:T(8,128)} %gather.10, f32[128,6]{1,0:T(8,128)S(1)} %copy.54), kind=kLoop, calls=%fused_computation.3 | loop fusion | flops 3604480 | bytes 9178112 | tf_op jit(solution)/shard_map/reduce_sum | solution.py:117
  340.4 0.7 fusion.11
  341.1 1.1 copy.58
  342.2 22.3 %reduce-scatter.4.cloned.1.call-done = bf16[640,128]{1,0:T(8,128)(2,1)} async-done(((bf16[2560,128]{1,0:T(8,128)(2,1)}), bf16[640,128]{1,0:T(8,128)(2,1)}) %reduce-scatter.4.cloned.1.call-update) | async-done | bytes 163856
  364.5 1.7 copy.59
  (46 shorter events, 1.7 us)
Async XLA Ops:
  6.5 147.5 %copy-start = (bf16[2,16,2560]{2,1,0:T(8,128)(2,1)S(1)}, bf16[2,16,2560]{2,1,0:T(8,128)(2,1)}, u32[]{:S(2)}) copy-start(bf16[2,16,2560]{2,1,0:T(8,128)(2,1)} %param.24) | copy-start | bytes 491524
  54.5 72.0 %copy-start.8 = (bf16[2,2560,384]{2,1,0:T(8,128)(2,1)S(1)}, bf16[2,2560,384]{2,1,0:T(8,128)(2,1)}, u32[]{:S(2)}) copy-start(bf16[2,2560,384]{2,1,0:T(8,128)(2,1)} %param.20) | copy-start | bytes 11796484
  124.3 2.3 copy-start.2
  147.6 5.1 %copy-start.4 = (bf16[2,768,16]{1,2,0:T(8,128)(2,1)S(1)}, bf16[2,768,16]{1,2,0:T(8,128)(2,1)}, u32[]{:S(2)}) copy-start(bf16[2,768,16]{1,2,0:T(8,128)(2,1)} %param.23) | copy-start | bytes 147460
  147.6 5.1 %copy-start.6 = (s32[16]{0:T(128)S(1)}, s32[16]{0:T(128)}, u32[]{:S(2)}) copy-start(s32[16]{0:T(128)} %param.25) | copy-start | bytes 196
  147.6 155.2 %all-to-all-start.1 = ((bf16[32,2,16,2560]{3,2,1,0:T(8,128)(2,1)}), bf16[32,2,16,2560]{3,2,1,0:T(8,128)(2,1)}, u32[]{:S(2)}, u32[]{:S(2)}) async-start(bf16[32,2,16,2560]{3,2,1,0:T(8,128)(2,1)} %copy.53), calls=%async_computation.1 | async-start | bytes 10485760 | tf_op jit(solution)/shard_map/all_to_all | solution.py:103
  152.6 3.5 copy-start.7
  152.6 3.9 %copy-start.10 = (s32[64]{0:T(128)S(1)}, s32[64]{0:T(128)}, u32[]{:S(2)}) copy-start(s32[64]{0:T(128)} %param.27) | copy-start | bytes 772
  152.6 4.0 %copy-start.5 = (f32[128,6]{0,1:T(8,128)S(1)}, f32[128,6]{0,1:T(8,128)}, u32[]{:S(2)}) copy-start(f32[128,6]{0,1:T(8,128)} %param.29) | copy-start | bytes 9220
  152.6 146.2 %all-reduce.3.cloned.1.call-start = ((), (), s32[]{:S(2)}) async-start(), calls=%async_computation.4 | async-start | bytes 3407872 | tf_op jit(solution)/shard_map/psum | solution.py:61
  155.8 208.7 %reduce-scatter.4.cloned.1.call-start = ((), (), s32[]{:S(2)}) async-start(), calls=%async_computation.3 | async-start | bytes 819200
  156.7 3.3 copy-start.9
  332.3 8.1 %copy-start.3 = (bf16[768,2560]{1,0:T(8,128)(2,1)S(1)}, bf16[768,2560]{1,0:T(8,128)(2,1)}, u32[]{:S(2)}) copy-start(bf16[768,2560]{1,0:T(8,128)(2,1)} %param.19) | copy-start | bytes 11796484
  332.3 33.9 %copy-start.1 = (bf16[2,16,2560]{2,1,0:T(8,128)(2,1)S(1)}, bf16[2,16,2560]{2,1,0:T(8,128)(2,1)}, u32[]{:S(2)}) copy-start(bf16[2,16,2560]{2,1,0:T(8,128)(2,1)} %param.24) | copy-start | bytes 491524
Sparse Core Ops, SparseCore 0:
  156.8 141.9 all-reduce.2
  342.4 22.1 reduce-scatter.3
where the time goes:
time: 374 us; the launch traced here: 373 us
  waiting for transfers between devices  160 us (43%)
  blocking collectives  84.6 us (23%)
  local copies, waits for them, and re-layouts  62.7 us (17%)
  matrix products  26.1 us (7%)
  other arithmetic  20.3 us (5%)
  between operations  13.6 us (4%)
  starting transfers between devices  5.31 us (1%)
    psum x1, waiting for transfers between devices, body(): lax.psum(picked_in, 'dp').astype(jnp.float32)  138 us
    all_to_all x1, blocking collectives, body(): lax.all_to_all(send_rows, 'dp', split_axis=0, concat_axis=0, tiled=True)  69.7 us
    scatter x1, local copies, waits for them, and re-layouts, body(): send_rows = jnp.zeros((total_experts * capacity, width), jnp.bfloat16).at...  27.6 us
    unnamed x3, waiting for transfers between devices  22.3 us
    gather x2, local copies, waits for them, and re-layouts, body(): picked_rows = returned[slot_index]  21.6 us
    all_gather x1, blocking collectives, body(): gathered = lax.all_gather(hidden, 'mp', axis=1, tiled=True)  14.9 us
    dot_general x1, matrix products, experts_apply(): jnp.einsum('sjcf,jfd->sjcd', inner, expert_down, preferred_element_type=j...  12.8 us
    reduce_sum x1, other arithmetic, body(): jnp.sum((picked_rows * flat_weights[:, None]).reshape(tok_rows, top_count...  8.08 us
  transfers between devices with their start and end apart: 3, of which 2 were waited for; matrix products, arithmetic and copies ran while one was open for 3% of the time, Pallas kernels for 0%

commit v1 on v0

--- a/solution.py
+++ b/solution.py
@@ -35,9 +35,27 @@
     dp_count = lax.axis_size("dp")
     mp_count = lax.axis_size("mp")
     dp_index = lax.axis_index("dp")
+    mp_index = lax.axis_index("mp")
     local_experts = expert_gate.shape[0]
     total_experts = local_experts * dp_count
     capacity = mp_count * max(1, tok_rows * top_count * 4 // (total_experts * mp_count * 3))
+    col_width = hidden.shape[1]
+    col_start = mp_index * col_width
+
+    active_count = active.shape[0]
+    rank_width = adapter_in.shape[2]
+    local_adapters = adapter_in.shape[0]
+    owned_ids = dp_index * local_adapters + jnp.arange(local_adapters, dtype=jnp.int32)
+    selector = (active[:, None] == owned_ids[None, :]).astype(jnp.bfloat16)
+    out_cols = lax.dynamic_slice_in_dim(adapter_out, col_start, col_width, axis=2)
+    picked_in = jnp.einsum(
+        "ji,isr->jsr", selector, adapter_in, preferred_element_type=jnp.float32
+    ).astype(jnp.bfloat16)
+    picked_out = jnp.einsum(
+        "ji,ird->jrd", selector, out_cols, preferred_element_type=jnp.float32
+    ).astype(jnp.bfloat16)
+    picked_in, picked_out = lax.psum((picked_in, picked_out), "dp")
+
     gathered = lax.all_gather(hidden, "mp", axis=1, tiled=True)
     values = gathered.astype(jnp.float32)
     factor = lax.rsqrt(jnp.mean(values * values, axis=-1, keepdims=True) + 1e-06)
@@ -46,22 +64,7 @@
     shared_lin = jnp.dot(normed, shared_gate, preferred_element_type=jnp.float32)
     shared_pre = jnp.dot(normed, shared_up, preferred_element_type=jnp.float32)
     shared_act = (jax.nn.silu(shared_lin) * shared_pre).astype(jnp.bfloat16)
-    active_count = active.shape[0]
-    rank_width = adapter_in.shape[2]
-    local_adapters = adapter_in.shape[0]
-    owned_ids = dp_index * local_adapters + jnp.arange(local_adapters, dtype=jnp.int32)
-    selector = (active[:, None] == owned_ids[None, :]).astype(jnp.bfloat16)
-    picked_in = jnp.einsum(
-        "ji,isr->jsr", selector, adapter_in, preferred_element_type=jnp.float32
-    ).astype(jnp.bfloat16)
-    picked_out = jnp.einsum(
-        "ji,ird->jrd", selector, adapter_out, preferred_element_type=jnp.float32
-    ).astype(jnp.bfloat16)
-    picked_in, picked_out = (
-        lax.psum(picked_in, "dp").astype(jnp.float32),
-        lax.psum(picked_out, "dp").astype(jnp.float32),
-    )
-    picked_in = picked_in.astype(jnp.bfloat16)
+
     request_end = jnp.cumsum(lengths)
     positions = dp_index * tok_rows + jnp.arange(tok_rows, dtype=jnp.int32)
     request_of = jnp.sum((request_end[None, :] <= positions[:, None]).astype(jnp.int32), axis=1)
@@ -76,29 +79,30 @@
         shared_act.shape[1], active_count * rank_width
     )
     lowrank = jnp.dot(shared_act, in_matrix, preferred_element_type=jnp.float32)
-    lowrank = (lowrank.reshape(tok_rows, active_count, rank_width) * chosen[:, :, None]).reshape(
+    lowrank_sel = jnp.sum(lowrank.reshape(tok_rows, active_count, rank_width) * chosen[:, :, None], axis=1)
+    lowrank_sel = lax.psum(lowrank_sel, "mp")
+    lowrank = (chosen[:, :, None] * lowrank_sel[:, None, :]).reshape(
         tok_rows, active_count * rank_width
     )
     adapted = jnp.dot(
         lowrank,
-        picked_out.reshape(active_count * rank_width, width),
+        picked_out.reshape(active_count * rank_width, col_width).astype(jnp.float32),
         precision=lax.Precision.HIGHEST,
     )
-    partial_out = jnp.dot(shared_act, shared_down, preferred_element_type=jnp.float32) + adapted
+
     flat_routes = routes.reshape(-1)
-    flat_weights = route_weights.reshape(-1)
     expert_hot = (
         flat_routes[:, None] == jnp.arange(total_experts, dtype=jnp.int32)[None, :]
     ).astype(jnp.int32)
     earlier = jnp.cumsum(expert_hot, axis=0) - expert_hot
     position = jnp.sum(earlier * expert_hot, axis=1)
-    slot_index = flat_routes * capacity + position
-    token_of = jnp.arange(tok_rows * top_count, dtype=jnp.int32) // top_count
-    send_rows = (
-        jnp.zeros((total_experts * capacity, width), jnp.bfloat16)
-        .at[slot_index]
-        .set(normed[token_of])
-    )
+    slot_index = (flat_routes * capacity + position).reshape(tok_rows, top_count)
+    slot_count = total_experts * capacity
+    slot_hit = slot_index[:, :, None] == jnp.arange(slot_count, dtype=jnp.int32)[None, None, :]
+    dispatch = jnp.any(slot_hit, axis=1).astype(jnp.bfloat16)
+    send_rows = jnp.einsum(
+        "ts,td->sd", dispatch, normed, preferred_element_type=jnp.float32
+    ).astype(jnp.bfloat16)
     send_rows = send_rows.reshape(dp_count, local_experts, capacity, width)
     returned = lax.all_to_all(
         experts_apply(
@@ -111,13 +115,20 @@
         split_axis=0,
         concat_axis=0,
         tiled=True,
-    ).astype(jnp.float32)
-    returned = returned.reshape(total_experts * capacity, width)
-    picked_rows = returned[slot_index]
-    routed = jnp.sum(
-        (picked_rows * flat_weights[:, None]).reshape(tok_rows, top_count, width), axis=1
     )
-    partial_out = partial_out + routed
+    returned = returned.reshape(slot_count, width)
+    combine = jnp.sum(
+        jnp.where(slot_hit, route_weights[:, :, None], 0.0), axis=1
+    )
+    combine_hi = combine.astype(jnp.bfloat16)
+    combine_lo = (combine - combine_hi.astype(jnp.float32)).astype(jnp.bfloat16)
+    routed = jnp.dot(combine_hi, returned, preferred_element_type=jnp.float32) + jnp.dot(
+        combine_lo, returned, preferred_element_type=jnp.float32
+    )
+
+    partial_out = jnp.dot(shared_act, shared_down, preferred_element_type=jnp.float32) + routed
+    own_cols = lax.dynamic_slice_in_dim(partial_out, col_start, col_width, axis=1) + adapted
+    partial_out = lax.dynamic_update_slice_in_dim(partial_out, own_cols, col_start, axis=1)
     return lax.psum_scatter(partial_out.astype(jnp.bfloat16), "mp", scatter_dimension=1, tiled=True)
 
 

time: 374 us -> 316 us (0.84)
  local copies, waits for them, and re-layouts: 62.7 us -> 14.3 us
  other arithmetic: 20.3 us -> 4.99 us
  blocking collectives: 84.6 us -> 95.2 us
  waiting for transfers between devices: 160 us -> 151 us
  matrix products: 26.1 us -> 31.9 us
    scatter x1 -> x0, local copies, waits for them, and re-layouts: 27.6 us -> none  [body(): send_rows = jnp.zeros((total_experts * capacity, width), jnp.bfloat16).at...]
    gather x2 -> x0, local copies, waits for them, and re-layouts: 21.6 us -> none  [body(): picked_rows = returned[slot_index]]
    psum x0 -> x1, blocking collectives: none -> 10.8 us  [body(): lowrank_sel = lax.psum(lowrank_sel, 'mp')]
    reshape x1 -> x0, other arithmetic: 7.93 us -> none  [body(): returned = returned.reshape(total_experts * capacity, width)]
    reduce_sum x1, other arithmetic: 8.08 us -> 0.41 us  [body(): jnp.sum(jnp.where(slot_hit, route_weights[:, :, None], 0.0), axis=1)]
    psum x1, waiting for transfers between devices: 138 us -> 131 us  [body(): picked_in, picked_out = lax.psum((picked_in, picked_out), 'dp')]
    dot_general x2 -> x5, matrix products: 4.36 us -> 9.96 us  [the longest x1 3.49 us: body(): jnp.dot(combine_lo, returned, preferred_element_type=jnp.float32)]
where the time goes in v1:
time: 316 us
  waiting for transfers between devices  151 us (48%)
  blocking collectives  95.2 us (30%)
  matrix products  31.9 us (10%)
  local copies, waits for them, and re-layouts  14.3 us (5%)
  between operations  13.7 us (4%)
  starting transfers between devices  5.27 us (2%)
  other arithmetic  4.99 us (2%)
    psum x1, waiting for transfers between devices, body(): picked_in, picked_out = lax.psum((picked_in, picked_out), 'dp')  131 us
    all_to_all x1, blocking collectives, body(): lax.all_to_all(send_rows, 'dp', split_axis=0, concat_axis=0, tiled=True)  69.5 us
    unnamed x3, waiting for transfers between devices  19.6 us
    all_gather x1, blocking collectives, body(): gathered = lax.all_gather(hidden, 'mp', axis=1, tiled=True)  14.9 us
    dot_general x1, matrix products, experts_apply(): jnp.einsum('sjcf,jfd->sjcd', inner, expert_down, preferred_element_type=j...  12.8 us
    psum x1, blocking collectives, body(): lowrank_sel = lax.psum(lowrank_sel, 'mp')  10.8 us
    unnamed x25, local copies, waits for them, and re-layouts  7.3 us
  transfers between devices with their start and end apart: 3, of which 2 were waited for; matrix products, arithmetic and copies ran while one was open for 3% of the time, Pallas kernels for 0%

profile of v1, /device:TPU:0, one launch (start us, length us, event | category | flops | bytes accessed | tf_op | source)
XLA Modules:
  0.0 315.9 jit_solution(4285871344129331172)
XLA Ops:
  6.5 0.8 copy.60
  7.7 1.8 reduce-window.18
  9.5 0.3 slice_reduce_fusion
  10.1 0.7 multiply_add_fusion
  10.8 0.5 fusion.9
  11.3 14.9 %all_gather.3 = bf16[128,2560]{1,0:T(8,128)(2,1)S(1)} all-gather(bf16[128,640]{1,0:T(8,128)(2,1)} %param.15), channel_id=1, replica_groups=mesh['dp'=32,'mp'=4] {'mp'}, dimensions={1}, use_global_device_ids=true | all-gather | bytes 819200 | tf_op jit(solution)/shard_map/all_gather | solution.py:59
  26.5 0.7 convert_element_type.64
  27.2 1.6 convolution_convert_fusion.1
  28.8 69.5 %all_to_all.10 = bf16[32,2,16,2560]{3,2,1,0:T(8,128)(2,1)S(1)} all-to-all(bf16[32,2,16,2560]{3,2,1,0:T(8,128)(2,1)S(1)} %bitcast.98), channel_id=1, replica_groups=mesh['dp'=32,'mp'=4] {'dp'}, dimensions={0} | all-to-all | bytes 10485760 | tf_op jit(solution)/shard_map/all_to_all | solution.py:109
  98.3 2.3 copy-done.1
  100.6 2.9 fusion.3
  103.5 12.8 %fusion = bf16[32,2,16,2560]{3,2,0,1:T(8,128)(2,1)} fusion(bf16[2,384,2560]{2,1,0:T(8,128)(2,1)} %param.22, f32[2,32,16,384]{3,2,1,0:T(8,128)S(1)} %fusion.3, bf16[2,2560,384]{2,1,0:T(8,128)(2,1)} %param.21, bf16[32,2,16,2560]{3,2,1,0:T(8,128)(2,1)} %copy-done.1), kind=kOutput, calls=%fused_computation.2 | convolution fusion | flops 4031512576 | bytes 19922944 | tf_op jit(solution)/shard_map/sjcf,jfd->sjcd/dot_general | solution.py:13
  116.3 5.3 %copy.66 = bf16[32,2,16,2560]{3,2,1,0:T(8,128)(2,1)} copy(bf16[32,2,16,2560]{3,2,0,1:T(8,128)(2,1)} %fusion) | data formatting | bytes 10485760 | tf_op jit(solution)/shard_map/convert_element_type | solution.py:113
  121.5 5.0 %all-to-all-start.1 = ((bf16[32,2,16,2560]{3,2,1,0:T(8,128)(2,1)}), bf16[32,2,16,2560]{3,2,1,0:T(8,128)(2,1)}, u32[]{:S(2)}, u32[]{:S(2)}) async-start(bf16[32,2,16,2560]{3,2,1,0:T(8,128)(2,1)} %copy.66), calls=%async_computation.1 | async-start | bytes 10485760 | tf_op jit(solution)/shard_map/all_to_all | solution.py:107
  126.6 0.4 fusion.25
  127.1 0.9 copy.95
  128.0 1.1 convolution_convert_fusion.3
  129.1 0.2 reduce-scatter.4.cloned.1.call-start
  129.9 0.4 select_reduce_fusion
  130.3 3.2 fusion.57
  133.5 0.8 fusion.26
  134.3 1.3 copy-done.2
  135.6 0.7 fusion.59
  136.3 131.0 %all-reduce.3.cloned.1.call-done = (bf16[16,16,640]{2,0,1:T(8,128)(2,1)}, bf16[16,16,768]{2,1,0:T(8,128)(2,1)}) async-done(((bf16[16,16,640]{2,0,1:T(8,128)(2,1)}, bf16[16,16,768]{2,1,0:T(8,128)(2,1)}), (bf16[16,16,640]{2,0,1:T(8,128)(2,1)}, bf16[16,16,768]{2,1,0:T(8,128)(2,1)})) %all-reduce.3.cloned.1.call-update) | async-done | bytes 720912 | tf_op jit(solution)/shard_map/psum | solution.py:57
  267.3 1.3 fusion.29
  268.6 10.8 %psum.22 = f32[128,16]{0,1:T(8,128)S(1)} all-reduce(f32[128,16]{0,1:T(8,128)S(1)} %fusion.29), channel_id=1, replica_groups=mesh['dp'=32,'mp'=4] {'mp'}, use_global_device_ids=true, to_apply=%region_11.12 | all-reduce | flops 2048 | bytes 16384 | tf_op jit(solution)/shard_map/psum | solution.py:83
  279.4 3.3 %fusion.39 = f32[128,2560]{1,0:T(8,128)S(1)} fusion(bf16[1024,2560]{1,0:T(8,128)(2,1)} %bitcast.11, f32[128,1024]{1,0:T(8,128)S(1)} %select_reduce_fusion), kind=kOutput, calls=%fused_computation.53 | convolution fusion | flops 671219712 | bytes 7077888 | tf_op jit(solution)/shard_map/dot_general | solution.py:125
  282.7 3.5 %fusion.8 = f32[128,2560]{1,0:T(8,128)S(1)} fusion(f32[128,2560]{1,0:T(8,128)S(1)} %fusion.59, f32[128,2560]{1,0:T(8,128)S(1)} %fusion.39, bf16[1024,2560]{1,0:T(8,128)(2,1)} %bitcast.11, f32[128,1024]{1,0:T(8,128)S(1)} %select_reduce_fusion), kind=kOutput, calls=%fused_computation.11 | convolution fusion | flops 672268288 | bytes 9699328 | tf_op jit(solution)/shard_map/dot_general | solution.py:125
  286.2 0.4 fusion.28
  286.7 1.1 copy.75
  287.8 19.6 %reduce-scatter.4.cloned.1.call-done = bf16[640,128]{1,0:T(8,128)(2,1)} async-done(((bf16[2560,128]{1,0:T(8,128)(2,1)}), bf16[640,128]{1,0:T(8,128)(2,1)}) %reduce-scatter.4.cloned.1.call-update) | async-done | bytes 163856
  307.4 1.7 copy.76
  (43 shorter events, 1.5 us)
Async XLA Ops:
  6.5 121.4 %copy-start = (bf16[2,16,2560]{2,1,0:T(8,128)(2,1)S(1)}, bf16[2,16,2560]{2,1,0:T(8,128)(2,1)}, u32[]{:S(2)}) copy-start(bf16[2,16,2560]{2,1,0:T(8,128)(2,1)} %param.24) | copy-start | bytes 491524
  28.8 71.8 %copy-start.8 = (bf16[2,2560,384]{2,1,0:T(8,128)(2,1)S(1)}, bf16[2,2560,384]{2,1,0:T(8,128)(2,1)}, u32[]{:S(2)}) copy-start(bf16[2,2560,384]{2,1,0:T(8,128)(2,1)} %param.20) | copy-start | bytes 11796484
  98.3 2.3 copy-start.1
  121.5 5.1 %copy-start.4 = (bf16[2,768,16]{1,2,0:T(8,128)(2,1)S(1)}, bf16[2,768,16]{1,2,0:T(8,128)(2,1)}, u32[]{:S(2)}) copy-start(bf16[2,768,16]{1,2,0:T(8,128)(2,1)} %param.23) | copy-start | bytes 147460
  121.5 5.1 %copy-start.6 = (s32[16]{0:T(128)S(1)}, s32[16]{0:T(128)}, u32[]{:S(2)}) copy-start(s32[16]{0:T(128)} %param.25) | copy-start | bytes 196
  121.5 7.8 %copy-start.7 = (s32[64]{0:T(128)S(1)}, s32[64]{0:T(128)}, u32[]{:S(2)}) copy-start(s32[64]{0:T(128)} %param.26) | copy-start | bytes 772
  121.5 8.2 %copy-start.10 = (s32[64]{0:T(128)S(1)}, s32[64]{0:T(128)}, u32[]{:S(2)}) copy-start(s32[64]{0:T(128)} %param.27) | copy-start | bytes 772
  121.5 8.3 %copy-start.5 = (f32[128,6]{0,1:T(8,128)S(1)}, f32[128,6]{0,1:T(8,128)}, u32[]{:S(2)}) copy-start(f32[128,6]{0,1:T(8,128)} %param.29) | copy-start | bytes 9220
  121.5 157.8 %all-to-all-start.1 = ((bf16[32,2,16,2560]{3,2,1,0:T(8,128)(2,1)}), bf16[32,2,16,2560]{3,2,1,0:T(8,128)(2,1)}, u32[]{:S(2)}, u32[]{:S(2)}) async-start(bf16[32,2,16,2560]{3,2,1,0:T(8,128)(2,1)} %copy.66), calls=%async_computation.1 | async-start | bytes 10485760 | tf_op jit(solution)/shard_map/all_to_all | solution.py:107
  126.6 140.7 %all-reduce.3.cloned.1.call-start = ((), (), s32[]{:S(2)}) async-start(), calls=%async_computation.4 | async-start | bytes 1441792 | tf_op jit(solution)/shard_map/psum | solution.py:57
  129.1 178.2 %reduce-scatter.4.cloned.1.call-start = ((), (), s32[]{:S(2)}) async-start(), calls=%async_computation.3 | async-start | bytes 819200
  129.7 3.8 %copy-start.9 = (bf16[2560,768]{1,0:T(8,128)(2,1)S(1)}, bf16[2560,768]{1,0:T(8,128)(2,1)}, u32[]{:S(2)}) copy-start(bf16[2560,768]{1,0:T(8,128)(2,1)} %param.18) | copy-start | bytes 11796484
  133.5 2.1 copy-start.2
  282.7 3.5 %copy-start.3 = (bf16[16,16,640]{2,0,1:T(8,128)(2,1)S(1)}, bf16[16,16,640]{2,0,1:T(8,128)(2,1)}, u32[]{:S(2)}) copy-start(bf16[16,16,640]{2,0,1:T(8,128)(2,1)} %get-tuple-element.5) | copy-start | bytes 983044
Sparse Core Ops, SparseCore 0:
  130.8 136.4 all-reduce.2
  287.9 19.4 reduce-scatter.3
